TPU v7x, 256 devices: a whole 4x4x8 slice. The times are simulated.
256 devices in a mesh: tile: 16 (over y, z_hi), spec: 16 (over x, z_lo, core).
Axes of the slice: x: 4, y: 4, z: 8 (z_hi: 4, z_lo: 2; z = z_hi * 2 + z_lo), core: 2. Of those that a mesh axis runs over, the one named last changes fastest.
Arguments:
- latent: bfloat16 [32, 4096, 1024], P(None, ('tile', 'spec')), may hold values from -6 to 6
- basis: bfloat16 [224, 32], replicated, may hold values from -1 to 1
- response: bfloat16 [8, 224], replicated, may hold values from -0.375 to 0.375
- hyper_obs: bfloat16 [224, 1024, 256], P('spec', 'tile'), may hold values from -6 to 6
- multi_obs: bfloat16 [8, 4096, 1024], P(None, ('tile', 'spec')), may hold values from -6 to 6
Outputs:
- z_next: bfloat16 [32, 4096, 1024], P(None, ('tile', 'spec'))
- hs_residual: bfloat16 [224, 1024, 256], P('spec', 'tile')
All inputs are finite; a program needn't handle non-finite values.
Results may differ from a plain program's by a relative error of at most 0.0054.
Values may be sent and summed in bfloat16 or wider, within the bound.
No kernel may reach another device: no remote copies, remote signals or barrier semaphores. Data moves between devices by JAX's collectives and lax.ppermute only.
A program may use at most 128 MiB of HBM per device.

v0:
```python
import jax
import jax.numpy as jnp
from jax import lax
from jax.sharding import PartitionSpec as P

DECIM = 4
HALO = 128
step_size = 0.3


def with_halo(cells, sides, width):
    for axis, dim in sides:
        count = lax.axis_size(axis)
        ends = count - 1
        head = lax.slice_in_dim(cells, 0, width, axis=dim)
        tail = lax.slice_in_dim(cells, cells.shape[dim] - width, cells.shape[dim], axis=dim)
        cells = jnp.concatenate(
            [
                lax.ppermute(tail, axis, [(i, (i + 1) % count) for i in range(ends)]),
                cells,
                lax.ppermute(head, axis, [((i + 1) % count, i) for i in range(ends)]),
            ],
            axis=dim,
        )
    return cells


def profile(where_at):
    narrow = DECIM / 2.0
    decay_len = 3.0 * HALO / 8.0
    ripple = jnp.cos(where_at * (jnp.pi / 7.0))
    return (
        jnp.exp(-where_at * where_at / (2.0 * narrow * narrow))
        + 0.5 * jnp.exp(-jnp.abs(where_at) / decay_len) * ripple * ripple
    )


def kernel_values(offsets):
    every_offset = jnp.arange(-HALO, HALO + 1).astype(jnp.float32)
    energy = jnp.sqrt(jnp.sum(profile(every_offset) ** 2))
    inside = jnp.abs(offsets) <= HALO
    return jnp.where(inside, profile(offsets.astype(jnp.float32)) / energy, 0.0).astype(
        jnp.bfloat16
    )


def banded(count, width, stride, shift):
    period = width + stride * count
    at = jnp.arange(period)
    offsets = jnp.where(at < width, at, at - period) + shift
    period_values = kernel_values(offsets)
    rows = jnp.tile(period_values, count)[: count * (period - stride)]
    return rows.reshape(count, period - stride)[:, :width]


def split_dot(spec, wide, narrow):
    high_wide = lax.reduce_precision(wide, exponent_bits=8, mantissa_bits=7)
    high = high_wide.astype(jnp.bfloat16)
    low = (wide - high_wide).astype(jnp.bfloat16)
    f32 = jnp.float32
    return jnp.einsum(spec, high, narrow, preferred_element_type=f32) + jnp.einsum(
        spec, low, narrow, preferred_element_type=f32
    )


def shards(latent, basis, response, hyper_obs, multi_obs):
    highest = lax.Precision.HIGHEST
    f32 = jnp.float32
    bf16 = jnp.bfloat16
    n_spec = lax.axis_size("spec")
    n_tile = lax.axis_size("tile")
    tile_index = lax.axis_index("tile")
    group, coarse_rows, coarse_cols = hyper_obs.shape
    rows_dev = coarse_rows * DECIM
    rim = HALO // DECIM
    subspace, rows_here, width_cols = latent.shape
    chunk = coarse_cols // n_spec
    wide_rows = coarse_rows + 2 * rim
    basis_wide = basis.astype(f32)
    column_t = banded(coarse_cols, width_cols, DECIM, 0)
    own_rows = banded(wide_rows, rows_dev, DECIM, HALO)
    cols_done = jnp.einsum(
        "qrc,sjc->sqjr",
        latent,
        column_t.reshape(n_spec, chunk, width_cols),
        preferred_element_type=f32,
    ).astype(bf16)
    tile_rows = lax.all_to_all(cols_done, "spec", split_axis=0, concat_axis=3, tiled=True)[0]
    obs_split = hyper_obs.reshape(group, coarse_rows, n_spec, chunk).transpose(2, 0, 3, 1)
    obs_cols = lax.all_to_all(obs_split, "spec", split_axis=0, concat_axis=1, tiled=True)[0]
    resp_basis = jnp.dot(response.astype(f32), basis_wide, precision=highest)
    multi_pred = jnp.einsum("mq,qrc->mrc", resp_basis, latent.astype(f32), precision=highest)
    multi_resid = (multi_pred - multi_obs.astype(f32)).astype(bf16)
    multi_resid, obs_cols = lax.optimization_barrier((multi_resid, obs_cols))
    obs_proj = jnp.einsum("bq,bji->qji", basis, obs_cols, preferred_element_type=f32)
    own_part = jnp.einsum("qjr,er->qje", tile_rows, own_rows, preferred_element_type=f32)
    half = wide_rows // 2
    ends = n_tile - 1
    to_next = jnp.concatenate(
        [
            lax.slice_in_dim(own_part, half, wide_rows, axis=2),
            lax.slice_in_dim(obs_proj, coarse_rows - rim, coarse_rows, axis=2),
        ],
        axis=2,
    )
    to_prev = jnp.concatenate(
        [lax.slice_in_dim(own_part, 0, half, axis=2), lax.slice_in_dim(obs_proj, 0, rim, axis=2)],
        axis=2,
    )
    got_prev = lax.ppermute(to_next, "tile", [(i, i + 1) for i in range(ends)])
    got_next = lax.ppermute(to_prev, "tile", [(i + 1, i) for i in range(ends)])
    coef_blurred = own_part + jnp.concatenate(
        [lax.slice_in_dim(got_prev, 0, half, axis=2), lax.slice_in_dim(got_next, 0, half, axis=2)],
        axis=2,
    )
    coef_own = lax.slice_in_dim(coef_blurred, rim, rim + coarse_rows, axis=2)
    blurred = split_dot("qji,bq->bji", coef_own, basis)
    resid_cols = (blurred - obs_cols.astype(f32)).astype(bf16)
    coef_resid = jnp.einsum("bq,bji->qji", basis, resid_cols, preferred_element_type=f32)
    gram = jnp.einsum("bq,bp->qp", basis, basis, preferred_element_type=f32)
    coef_rim = jnp.concatenate(
        [
            lax.slice_in_dim(coef_blurred, 0, rim, axis=2),
            lax.slice_in_dim(coef_blurred, wide_rows - rim, wide_rows, axis=2),
        ],
        axis=2,
    )
    proj_rim = jnp.concatenate(
        [
            lax.slice_in_dim(got_prev, half, half + rim, axis=2),
            lax.slice_in_dim(got_next, half, half + rim, axis=2),
        ],
        axis=2,
    )
    resid_rim = jnp.einsum("qp,pji->qji", gram, coef_rim, precision=highest) - proj_rim
    rim_prev = jnp.where(tile_index > 0, lax.slice_in_dim(resid_rim, 0, rim, axis=2), 0.0)
    rim_next = jnp.where(tile_index < ends, lax.slice_in_dim(resid_rim, rim, 2 * rim, axis=2), 0.0)
    coef_wide = jnp.concatenate([rim_prev, coef_resid, rim_next], axis=2)
    back_split = split_dot(
        "qjk,ksr->sqrj", coef_wide, own_rows.reshape(wide_rows, n_spec, rows_here)
    ).astype(bf16)
    rows_pixel = lax.all_to_all(back_split, "spec", split_axis=0, concat_axis=3, tiled=True)[0]
    grad_hs = jnp.einsum("qrj,jc->qrc", rows_pixel, column_t, preferred_element_type=f32)
    resid_split = resid_cols.reshape(n_spec, group, chunk, coarse_rows)
    resid_split, _ = lax.optimization_barrier((resid_split, rows_pixel))
    resid_bands = lax.all_to_all(resid_split, "spec", split_axis=0, concat_axis=2, tiled=True)[0]
    hs_residual = resid_bands.transpose(0, 2, 1)
    grad_ms = jnp.einsum("mq,mrc->qrc", resp_basis, multi_resid.astype(f32), precision=highest)
    gradient = grad_hs + grad_ms
    z_next = (latent.astype(f32) - step_size * gradient).astype(bf16)
    return (z_next, hs_residual)


def solution(mesh):
    in_specs = (
        P(None, ("tile", "spec"), None),
        P(),
        P(),
        P("spec", "tile", None),
        P(None, ("tile", "spec"), None),
    )
    out_specs = (P(None, ("tile", "spec"), None), P("spec", "tile", None))
    return jax.shard_map(shards, mesh=mesh, in_specs=in_specs, out_specs=out_specs, check_vma=False)
```

profile of v0, /device:TPU:24, one launch (start us, length us, event | category | flops | bytes accessed | tf_op | source)
XLA Modules:
  0.0 100.2 jit_solution(10661442841546105906)
XLA Ops:
  2.6 1.7 %reshape.88 = bf16[256,2044]{1,0:T(8,128)(2,1)S(1)} reshape(bf16[523264]{0:T(1024)(128)(2,1)S(1)} %slice.70) | data formatting | bytes 2093056 | tf_op jit(solution)/shard_map/reshape | solution.py:53
  4.3 1.4 %fusion.55 = bf16[16,16,16,32]{3,2,1,0:T(8,128)(2,1)S(1)} fusion(bf16[16,16,1024,1]{2,1,3,0:T(8,128)(2,1)S(1)} %bitcast.123, bf16[32,16,1024]{2,1,0:T(8,128)(2,1)S(1)} %copy-done.1), kind=kOutput, calls=%fused_computation.85 | convolution fusion | flops 268566528 | bytes 1835008 | tf_op jit(solution)/shard_map/qrc,sjc->sqjr/dot_general | solution.py:82
  5.8 1.7 %reshape.104 = bf16[16,2,4096]{2,1,0:T(2,128)(2,1)} reshape(bf16[16,16,16,32]{3,2,1,0:T(8,128)(2,1)S(1)} %fusion.55) | data formatting | bytes 524288
  7.4 5.8 %all-to-all-start = ((bf16[16,2,4096]{2,1,0:T(2,128)(2,1)}), bf16[16,2,4096]{2,1,0:T(2,128)(2,1)S(1)}, u32[]{:S(2)}, u32[]{:S(2)}) async-start(bf16[16,2,4096]{2,1,0:T(2,128)(2,1)} %reshape.104), calls=%async_computation | async-start | bytes 524288 | tf_op jit(solution)/shard_map/all_to_all | solution.py:88
  14.0 1.5 %copy.50 = bf16[14,64,256]{1,2,0:T(8,128)(2,1)S(1)} copy(bf16[14,64,256]{2,1,0:T(8,128)(2,1)} %param.8) | data formatting | bytes 917504 | tf_op args[3]
  15.7 1.3 %reshape.102 = bf16[16,2,7168]{2,1,0:T(2,128)(2,1)} reshape(bf16[16,14,16,64]{3,2,1,0:T(8,128)(2,1)S(1)} %copy.51) | data formatting | bytes 917504
  17.0 4.3 %all-to-all-done = bf16[16,2,4096]{2,1,0:T(2,128)(2,1)S(1)} async-done(((bf16[16,2,4096]{2,1,0:T(2,128)(2,1)}), bf16[16,2,4096]{2,1,0:T(2,128)(2,1)S(1)}, u32[]{:S(2)}, u32[]{:S(2)}) %all-to-all-start) | async-done | bytes 262176 | tf_op jit(solution)/shard_map/all_to_all | solution.py:88
  21.3 3.6 %all-to-all-start.1 = ((bf16[16,2,7168]{2,1,0:T(2,128)(2,1)}), bf16[16,2,7168]{2,1,0:T(2,128)(2,1)S(1)}, u32[]{:S(2)}, u32[]{:S(2)}) async-start(bf16[16,2,7168]{2,1,0:T(2,128)(2,1)} %reshape.102), calls=%async_computation.1 | async-start | bytes 917504 | tf_op jit(solution)/shard_map/all_to_all | solution.py:90
  25.0 3.2 %fusion.8 = bf16[8,16,1024]{2,0,1:T(8,128)(2,1)} fusion(f32[8,32,1]{1,0,2:T(8,128)S(1)} %convolution_bitcast_fusion.2, bf16[32,16,1024]{2,1,0:T(8,128)(2,1)S(1)} %copy-done.1, bf16[8,16,1024]{2,1,0:T(8,128)(2,1)} %param.9), kind=kOutput, calls=%fused_computation.13 | convolution fusion | flops 50724864 | bytes 1573888 | tf_op jit(solution)/shard_map/mq,qrc->mrc/dot_general | solution.py:92
  30.8 4.1 %all-to-all-done.1 = bf16[16,2,7168]{2,1,0:T(2,128)(2,1)S(1)} async-done(((bf16[16,2,7168]{2,1,0:T(2,128)(2,1)}), bf16[16,2,7168]{2,1,0:T(2,128)(2,1)S(1)}, u32[]{:S(2)}, u32[]{:S(2)}) %all-to-all-start.1) | async-done | bytes 458784 | tf_op jit(solution)/shard_map/all_to_all | solution.py:90
  37.1 7.5 %collective-permute-start.1 = (f32[32,16,96]{2,1,0:T(8,128)S(1)}, f32[32,16,96]{2,1,0:T(8,128)S(1)}, u32[]{:S(2)}, u32[]{:S(2)}) collective-permute-start(f32[32,16,96]{2,1,0:T(8,128)S(1)} %pad_maximum_fusion.1), channel_id=1, source_target_pairs={{16,0},{32,16},{48,32},{64,48},{80,64},{96,80},{112,96},{128,112},... | collective-permute-start | bytes 589832 | tf_op jit(solution)/shard_map/ppermute | solution.py:111
  44.7 2.1 %collective-permute-start = (f32[32,16,96]{2,1,0:T(8,128)S(1)}, f32[32,16,96]{2,1,0:T(8,128)S(1)}, u32[]{:S(2)}, u32[]{:S(2)}) collective-permute-start(f32[32,16,96]{2,1,0:T(8,128)S(1)} %pad_maximum_fusion), channel_id=1, source_target_pairs={{0,16},{16,32},{32,48},{48,64},{64,80},{80,96},{96,112},{112,128},... | collective-permute-start | bytes 589832 | tf_op jit(solution)/shard_map/ppermute | solution.py:110
  47.1 8.2 %collective-permute-done.1 = f32[32,16,96]{2,1,0:T(8,128)S(1)} collective-permute-done((f32[32,16,96]{2,1,0:T(8,128)S(1)}, f32[32,16,96]{2,1,0:T(8,128)S(1)}, u32[]{:S(2)}, u32[]{:S(2)}) %collective-permute-start.1) | collective-permute-done | bytes 196640 | tf_op jit(solution)/shard_map/ppermute | solution.py:111
  55.3 7.2 %collective-permute-done = f32[32,16,96]{2,1,0:T(8,128)S(1)} collective-permute-done((f32[32,16,96]{2,1,0:T(8,128)S(1)}, f32[32,16,96]{2,1,0:T(8,128)S(1)}, u32[]{:S(2)}, u32[]{:S(2)}) %collective-permute-start) | collective-permute-done | bytes 196640 | tf_op jit(solution)/shard_map/ppermute | solution.py:110
  66.5 1.7 %reshape.106 = bf16[16,2,4096]{2,1,0:T(2,128)(2,1)} reshape(bf16[16,16,16,32]{3,2,1,0:T(8,128)(2,1)S(1)} %fusion.58) | data formatting | bytes 524288
  68.1 3.5 %all-to-all-start.2 = ((bf16[16,2,4096]{2,1,0:T(2,128)(2,1)}), bf16[16,2,4096]{2,1,0:T(2,128)(2,1)S(1)}, u32[]{:S(2)}, u32[]{:S(2)}) async-start(bf16[16,2,4096]{2,1,0:T(2,128)(2,1)} %reshape.106), calls=%async_computation.2 | async-start | bytes 524288 | tf_op jit(solution)/shard_map/all_to_all | solution.py:142
  72.5 7.2 %all-to-all-done.2 = bf16[16,2,4096]{2,1,0:T(2,128)(2,1)S(1)} async-done(((bf16[16,2,4096]{2,1,0:T(2,128)(2,1)}), bf16[16,2,4096]{2,1,0:T(2,128)(2,1)S(1)}, u32[]{:S(2)}, u32[]{:S(2)}) %all-to-all-start.2) | async-done | bytes 262176 | tf_op jit(solution)/shard_map/all_to_all | solution.py:142
  79.7 1.5 %reshape.107 = bf16[16,16,16,32]{3,2,1,0:T(8,128)(2,1)} reshape(bf16[16,2,4096]{2,1,0:T(2,128)(2,1)S(1)} %all-to-all-done.2) | data formatting | bytes 524288
  81.2 1.3 %reshape.108 = bf16[16,2,7168]{2,1,0:T(2,128)(2,1)} reshape(bf16[16,14,16,64]{3,2,1,0:T(8,128)(2,1)S(1)} %bitcast.115) | data formatting | bytes 917504
  82.4 4.2 %all-to-all-start.3 = ((bf16[16,2,7168]{2,1,0:T(2,128)(2,1)}), bf16[16,2,7168]{2,1,0:T(2,128)(2,1)}, u32[]{:S(2)}, u32[]{:S(2)}) async-start(bf16[16,2,7168]{2,1,0:T(2,128)(2,1)} %reshape.108), calls=%async_computation.3 | async-start | bytes 917504 | tf_op jit(solution)/shard_map/all_to_all | solution.py:146
  87.7 2.4 %copy.61 = bf16[32,16,256]{2,1,0:T(8,128)(2,1)S(1)} copy(bf16[32,16,256]{0,1,2:T(8,128)(2,1)} %bitcast.109) | data formatting | bytes 524288 | tf_op jit(solution)/shard_map/squeeze | solution.py:142
  90.1 3.4 %fusion.2 = bf16[32,16,1024]{2,1,0:T(8,128)(2,1)} fusion(f32[32,16,1024]{2,0,1:T(8,128)S(1)} %fusion.61, bf16[32,16,1024]{2,1,0:T(8,128)(2,1)S(1)} %copy-done.1, bf16[32,16,256]{2,1,0:T(8,128)(2,1)S(1)} %copy.61, bf16[256,2044]{1,0:T(8,128)(2,1)} %copy-done.2), kind=kOutput, calls=%fused_computation.3 | convolution fusion | flops 271056896 | bytes 4980736 | tf_op jit(solution)/shard_map/qrj,jc->qrc/dot_general | solution.py:143
  93.6 3.3 %all-to-all-done.3 = bf16[16,2,7168]{2,1,0:T(2,128)(2,1)} async-done(((bf16[16,2,7168]{2,1,0:T(2,128)(2,1)}), bf16[16,2,7168]{2,1,0:T(2,128)(2,1)}, u32[]{:S(2)}, u32[]{:S(2)}) %all-to-all-start.3) | async-done | bytes 458784 | tf_op jit(solution)/shard_map/all_to_all | solution.py:146
  96.8 2.1 %reshape.109 = bf16[16,14,16,64]{3,2,1,0:T(8,128)(2,1)S(1)} reshape(bf16[16,2,7168]{2,1,0:T(2,128)(2,1)} %all-to-all-done.3) | data formatting | bytes 917504
  (65 shorter events, 14.2 us)
Async XLA Ops:
  0.6 24.2 %copy-start = (bf16[224,32]{0,1:T(8,128)(2,1)S(1)}, bf16[224,32]{0,1:T(8,128)(2,1)}, u32[]{:S(2)}) copy-start(bf16[224,32]{0,1:T(8,128)(2,1)} %param.6) | copy-start | bytes 43012
  2.5 1.8 %copy-start.1 = (bf16[32,16,1024]{2,1,0:T(8,128)(2,1)S(1)}, bf16[32,16,1024]{2,1,0:T(8,128)(2,1)}, u32[]{:S(2)}) copy-start(bf16[32,16,1024]{2,1,0:T(8,128)(2,1)} %param.5) | copy-start | bytes 3145732
  4.3 1.5 %copy-start.2 = (bf16[256,2044]{1,0:T(8,128)(2,1)}, bf16[256,2044]{1,0:T(8,128)(2,1)S(1)}, u32[]{:S(2)}) copy-start(bf16[256,2044]{1,0:T(8,128)(2,1)S(1)} %reshape.88) | copy-start | bytes 3139588
  7.4 13.8 %all-to-all-start = ((bf16[16,2,4096]{2,1,0:T(2,128)(2,1)}), bf16[16,2,4096]{2,1,0:T(2,128)(2,1)S(1)}, u32[]{:S(2)}, u32[]{:S(2)}) async-start(bf16[16,2,4096]{2,1,0:T(2,128)(2,1)} %reshape.104), calls=%async_computation | async-start | bytes 524288 | tf_op jit(solution)/shard_map/all_to_all | solution.py:88
  14.0 15.8 %copy-start.5 = (bf16[128,764]{1,0:T(8,128)(2,1)}, bf16[128,764]{1,0:T(8,128)(2,1)S(1)}, u32[]{:S(2)}) copy-start(bf16[128,764]{1,0:T(8,128)(2,1)S(1)} %reshape.86) | copy-start | bytes 586756
  15.5 9.4 %copy-start.8 = (bf16[8,224]{1,0:T(8,128)(2,1)S(1)}, bf16[8,224]{1,0:T(8,128)(2,1)}, u32[]{:S(2)}) copy-start(bf16[8,224]{1,0:T(8,128)(2,1)} %param.7) | copy-start | bytes 10756
  21.3 13.7 %all-to-all-start.1 = ((bf16[16,2,7168]{2,1,0:T(2,128)(2,1)}), bf16[16,2,7168]{2,1,0:T(2,128)(2,1)S(1)}, u32[]{:S(2)}, u32[]{:S(2)}) async-start(bf16[16,2,7168]{2,1,0:T(2,128)(2,1)} %reshape.102), calls=%async_computation.1 | async-start | bytes 917504 | tf_op jit(solution)/shard_map/all_to_all | solution.py:90
  25.0 4.8 %copy-start.6 = (f32[8,32,1]{1,0,2:T(8,128)}, f32[8,32,1]{1,0,2:T(8,128)S(1)}, u32[]{:S(2)}) copy-start(f32[8,32,1]{1,0,2:T(8,128)S(1)} %convolution_bitcast_fusion.2) | copy-start | bytes 3076
  35.5 1.4 %copy-start.4 = (f32[32,16,64]{2,1,0:T(8,128)S(1)}, f32[32,16,64]{2,1,0:T(8,128)}, u32[]{:S(2)}) copy-start(f32[32,16,64]{2,1,0:T(8,128)} %get-tuple-element.19) | copy-start | bytes 393220
  36.3 10.6 %slice-start = ((bf16[128,764]{1,0:T(8,128)(2,1)}), bf16[128,256]{1,0:T(8,128)(2,1)S(1)}, s32[]{:S(2)}) async-start(bf16[128,764]{1,0:T(8,128)(2,1)} %copy-done.5), calls=%async_computation.4 | async-start | bytes 131072 | tf_op jit(solution)/shard_map/slice | solution.py:53
  37.1 18.2 %collective-permute-start.1 = (f32[32,16,96]{2,1,0:T(8,128)S(1)}, f32[32,16,96]{2,1,0:T(8,128)S(1)}, u32[]{:S(2)}, u32[]{:S(2)}) collective-permute-start(f32[32,16,96]{2,1,0:T(8,128)S(1)} %pad_maximum_fusion.1), channel_id=1, source_target_pairs={{16,0},{32,16},{48,32},{64,48},{80,64},{96,80},{112,96},{128,112},... | collective-permute-start | bytes 589832 | tf_op jit(solution)/shard_map/ppermute | solution.py:111
  44.7 17.8 %collective-permute-start = (f32[32,16,96]{2,1,0:T(8,128)S(1)}, f32[32,16,96]{2,1,0:T(8,128)S(1)}, u32[]{:S(2)}, u32[]{:S(2)}) collective-permute-start(f32[32,16,96]{2,1,0:T(8,128)S(1)} %pad_maximum_fusion), channel_id=1, source_target_pairs={{0,16},{16,32},{32,48},{48,64},{64,80},{80,96},{96,112},{112,128},... | collective-permute-start | bytes 589832 | tf_op jit(solution)/shard_map/ppermute | solution.py:110
  68.1 11.6 %all-to-all-start.2 = ((bf16[16,2,4096]{2,1,0:T(2,128)(2,1)}), bf16[16,2,4096]{2,1,0:T(2,128)(2,1)S(1)}, u32[]{:S(2)}, u32[]{:S(2)}) async-start(bf16[16,2,4096]{2,1,0:T(2,128)(2,1)} %reshape.106), calls=%async_computation.2 | async-start | bytes 524288 | tf_op jit(solution)/shard_map/all_to_all | solution.py:142
  72.5 14.2 %copy-start.3 = (bf16[8,16,1024]{2,0,1:T(8,128)(2,1)S(1)}, bf16[8,16,1024]{2,0,1:T(8,128)(2,1)}, u32[]{:S(2)}) copy-start(bf16[8,16,1024]{2,0,1:T(8,128)(2,1)} %fusion.8) | copy-start | bytes 786436
  72.5 14.2 %copy-start.7 = (f32[8,32,1]{1,0,2:T(8,128)S(1)}, f32[8,32,1]{1,0,2:T(8,128)}, u32[]{:S(2)}) copy-start(f32[8,32,1]{1,0,2:T(8,128)} %copy-done.6) | copy-start | bytes 3076
  82.4 14.4 %all-to-all-start.3 = ((bf16[16,2,7168]{2,1,0:T(2,128)(2,1)}), bf16[16,2,7168]{2,1,0:T(2,128)(2,1)}, u32[]{:S(2)}, u32[]{:S(2)}) async-start(bf16[16,2,7168]{2,1,0:T(2,128)(2,1)} %reshape.108), calls=%async_computation.3 | async-start | bytes 917504 | tf_op jit(solution)/shard_map/all_to_all | solution.py:146
where the time goes:
time: 101 us; the launch traced here: 100 us
  waiting for transfers between devices  34.4 us (34%)
  starting transfers between devices  26.7 us (26%)
  local copies, waits for them, and re-layouts  23.2 us (23%)
  matrix products  12.4 us (12%)
  between operations  1.83 us (2%)
  other arithmetic  1.81 us (2%)
    unnamed x30, local copies, waits for them, and re-layouts  13.6 us
    ppermute x1, waiting for transfers between devices, shards(): got_next = lax.ppermute(to_prev, 'tile', [(i + 1, i) for i in range(ends)])  8.2 us
    ppermute x1, starting transfers between devices, shards(): got_next = lax.ppermute(to_prev, 'tile', [(i + 1, i) for i in range(ends)])  7.49 us
    ppermute x1, waiting for transfers between devices, shards(): got_prev = lax.ppermute(to_next, 'tile', [(i, i + 1) for i in range(ends)])  7.23 us
    all_to_all x1, waiting for transfers between devices, shards(): lax.all_to_all(back_split, 'spec', split_axis=0, concat_axis=3, tiled=True)  7.21 us
    all_to_all x1, starting transfers between devices, shards(): lax.all_to_all(cols_done, 'spec', split_axis=0, concat_axis=3, tiled=True)  5.76 us
    all_to_all x1, waiting for transfers between devices, shards(): lax.all_to_all(cols_done, 'spec', split_axis=0, concat_axis=3, tiled=True)  4.31 us
    all_to_all x1, starting transfers between devices, shards(): lax.all_to_all(resid_split, 'spec', split_axis=0, concat_axis=2, tiled=True)  4.22 us
  transfers between devices with their start and end apart: 6, of which 6 were waited for; matrix products, arithmetic and copies ran while one was open for 18% of the time, Pallas kernels for 0%

commit v1 on v0

--- a/solution.py
+++ b/solution.py
@@ -64,6 +64,14 @@
 
 
 def shards(latent, basis, response, hyper_obs, multi_obs):
+
+    def extend_the_view(local):
+        arr_out = jnp.concatenate(
+            lax.all_to_all(jnp.stack(jnp.split(local, lax.axis_size("spec"), 0), 0), "spec", 0, 0),
+            1,
+        )
+        return arr_out
+
     highest = lax.Precision.HIGHEST
     f32 = jnp.float32
     bf16 = jnp.bfloat16
@@ -87,7 +95,7 @@
     ).astype(bf16)
     tile_rows = lax.all_to_all(cols_done, "spec", split_axis=0, concat_axis=3, tiled=True)[0]
     obs_split = hyper_obs.reshape(group, coarse_rows, n_spec, chunk).transpose(2, 0, 3, 1)
-    obs_cols = lax.all_to_all(obs_split, "spec", split_axis=0, concat_axis=1, tiled=True)[0]
+    obs_cols = extend_the_view(obs_split)[0]
     resp_basis = jnp.dot(response.astype(f32), basis_wide, precision=highest)
     multi_pred = jnp.einsum("mq,qrc->mrc", resp_basis, latent.astype(f32), precision=highest)
     multi_resid = (multi_pred - multi_obs.astype(f32)).astype(bf16)

time: 101 us -> 103 us (1.020)
  other arithmetic: 1.81 us -> 3.47 us
    unnamed x30 -> x43, local copies, waits for them, and re-layouts: 13.6 us -> 13.8 us
  transfers between devices with their start and end apart: 6 -> 6, of which waited for: 6 -> 6; matrix products, arithmetic and copies ran while one was open for 18% -> 17% of each run, Pallas kernels for 0% -> 0%
where the time goes in v1:
time: 103 us; the launch traced here: 102 us
  waiting for transfers between devices  35.1 us (34%)
  starting transfers between devices  26.7 us (26%)
  local copies, waits for them, and re-layouts  23.3 us (23%)
  matrix products  11.7 us (11%)
  other arithmetic  3.47 us (3%)
  between operations  1.87 us (2%)
    unnamed x43, local copies, waits for them, and re-layouts  13.8 us
    ppermute x1, waiting for transfers between devices, shards(): got_prev = lax.ppermute(to_next, 'tile', [(i, i + 1) for i in range(ends)])  8.14 us
    ppermute x1, waiting for transfers between devices, shards(): got_next = lax.ppermute(to_prev, 'tile', [(i + 1, i) for i in range(ends)])  7.5 us
    ppermute x1, starting transfers between devices, shards(): got_next = lax.ppermute(to_prev, 'tile', [(i + 1, i) for i in range(ends)])  7.49 us
    all_to_all x1, waiting for transfers between devices, shards(): lax.all_to_all(back_split, 'spec', split_axis=0, concat_axis=3, tiled=True)  7.23 us
    all_to_all x1, starting transfers between devices, shards(): lax.all_to_all(cols_done, 'spec', split_axis=0, concat_axis=3, tiled=True)  5.76 us
    all_to_all x1, waiting for transfers between devices, extend_the_view(): lax.all_to_all(jnp.stack(jnp.split(local, lax.axis_size('spec'), 0), 0),...  4.76 us
    all_to_all x1, starting transfers between devices, shards(): lax.all_to_all(resid_split, 'spec', split_axis=0, concat_axis=2, tiled=True)  4.22 us
  transfers between devices with their start and end apart: 6, of which 6 were waited for; matrix products, arithmetic and copies ran while one was open for 17% of the time, Pallas kernels for 0%

profile of v1, /device:TPU:24, one launch (start us, length us, event | category | flops | bytes accessed | tf_op | source)
XLA Modules:
  0.0 102.1 jit_solution(7778482799966785292)
XLA Ops:
  2.6 1.7 %reshape.84 = bf16[256,2044]{1,0:T(8,128)(2,1)S(1)} reshape(bf16[523264]{0:T(1024)(128)(2,1)S(1)} %slice.70) | data formatting | bytes 2093056 | tf_op jit(solution)/shard_map/reshape | solution.py:53
  4.3 1.4 %fusion.71 = bf16[16,16,16,32]{3,2,1,0:T(8,128)(2,1)S(1)} fusion(bf16[16,16,1024,1]{2,1,3,0:T(8,128)(2,1)S(1)} %bitcast.230, bf16[32,16,1024]{2,1,0:T(8,128)(2,1)S(1)} %copy-done.1), kind=kOutput, calls=%fused_computation.117 | convolution fusion | flops 268566528 | bytes 1835008 | tf_op jit(solution)/shard_map/qrc,sjc->sqjr/dot_general | solution.py:90
  5.8 1.7 %reshape.100 = bf16[16,2,4096]{2,1,0:T(2,128)(2,1)} reshape(bf16[16,16,16,32]{3,2,1,0:T(8,128)(2,1)S(1)} %fusion.71) | data formatting | bytes 524288
  7.4 5.8 %all-to-all-start = ((bf16[16,2,4096]{2,1,0:T(2,128)(2,1)}), bf16[16,2,4096]{2,1,0:T(2,128)(2,1)S(1)}, u32[]{:S(2)}, u32[]{:S(2)}) async-start(bf16[16,2,4096]{2,1,0:T(2,128)(2,1)} %reshape.100), calls=%async_computation | async-start | bytes 524288 | tf_op jit(solution)/shard_map/all_to_all | solution.py:96
  13.2 1.4 %copy.44 = bf16[14,64,256]{1,2,0:T(8,128)(2,1)S(1)} copy(bf16[14,64,256]{2,1,0:T(8,128)(2,1)} %param.8) | data formatting | bytes 917504 | tf_op args[3]
  15.0 1.3 %reshape.98 = bf16[16,2,7168]{2,1,0:T(2,128)(2,1)} reshape(bf16[16,1,14,16,64]{4,3,2,1,0:T(8,128)(2,1)S(1)} %fusion.27) | data formatting | bytes 917504
  17.1 4.2 %all-to-all-done = bf16[16,2,4096]{2,1,0:T(2,128)(2,1)S(1)} async-done(((bf16[16,2,4096]{2,1,0:T(2,128)(2,1)}), bf16[16,2,4096]{2,1,0:T(2,128)(2,1)S(1)}, u32[]{:S(2)}, u32[]{:S(2)}) %all-to-all-start) | async-done | bytes 262176 | tf_op jit(solution)/shard_map/all_to_all | solution.py:96
  21.3 3.6 %all-to-all-start.1 = ((bf16[16,2,7168]{2,1,0:T(2,128)(2,1)}), bf16[16,2,7168]{2,1,0:T(2,128)(2,1)S(1)}, u32[]{:S(2)}, u32[]{:S(2)}) async-start(bf16[16,2,7168]{2,1,0:T(2,128)(2,1)} %reshape.98), calls=%async_computation.1 | async-start | bytes 917504 | tf_op jit(solution)/shard_map/all_to_all | solution.py:70
  25.0 2.5 %fusion.8 = bf16[8,16,1024]{2,0,1:T(8,128)(2,1)S(1)} fusion(f32[8,32,1]{1,0,2:T(8,128)S(1)} %convolution_bitcast_fusion.2, bf16[32,16,1024]{2,1,0:T(8,128)(2,1)S(1)} %copy-done.1, bf16[8,16,1024]{2,1,0:T(8,128)(2,1)} %param.9), kind=kOutput, calls=%fused_computation.13 | convolution fusion | flops 50724864 | bytes 1573888 | tf_op jit(solution)/shard_map/mq,qrc->mrc/dot_general | solution.py:100
  30.2 4.8 %all-to-all-done.1 = bf16[16,2,7168]{2,1,0:T(2,128)(2,1)S(1)} async-done(((bf16[16,2,7168]{2,1,0:T(2,128)(2,1)}), bf16[16,2,7168]{2,1,0:T(2,128)(2,1)S(1)}, u32[]{:S(2)}, u32[]{:S(2)}) %all-to-all-start.1) | async-done | bytes 458784 | tf_op jit(solution)/shard_map/all_to_all | solution.py:70
  38.0 7.5 %collective-permute-start.1 = (f32[32,16,96]{2,1,0:T(8,128)S(1)}, f32[32,16,96]{2,1,0:T(8,128)S(1)}, u32[]{:S(2)}, u32[]{:S(2)}) collective-permute-start(f32[32,16,96]{2,1,0:T(8,128)S(1)} %pad_maximum_fusion.1), channel_id=1, source_target_pairs={{16,0},{32,16},{48,32},{64,48},{80,64},{96,80},{112,96},{128,112},... | collective-permute-start | bytes 589832 | tf_op jit(solution)/shard_map/ppermute | solution.py:119
  46.4 2.1 %collective-permute-start = (f32[32,16,96]{2,1,0:T(8,128)}, f32[32,16,96]{2,1,0:T(8,128)S(1)}, u32[]{:S(2)}, u32[]{:S(2)}) collective-permute-start(f32[32,16,96]{2,1,0:T(8,128)} %pad_maximum_fusion), channel_id=1, source_target_pairs={{0,16},{16,32},{32,48},{48,64},{64,80},{80,96},{96,112},{112,128},... | collective-permute-start | bytes 589832 | tf_op jit(solution)/shard_map/ppermute | solution.py:118
  48.7 7.5 %collective-permute-done.1 = f32[32,16,96]{2,1,0:T(8,128)S(1)} collective-permute-done((f32[32,16,96]{2,1,0:T(8,128)S(1)}, f32[32,16,96]{2,1,0:T(8,128)S(1)}, u32[]{:S(2)}, u32[]{:S(2)}) %collective-permute-start.1) | collective-permute-done | bytes 196640 | tf_op jit(solution)/shard_map/ppermute | solution.py:119
  56.2 8.1 %collective-permute-done = f32[32,16,96]{2,1,0:T(8,128)S(1)} collective-permute-done((f32[32,16,96]{2,1,0:T(8,128)}, f32[32,16,96]{2,1,0:T(8,128)S(1)}, u32[]{:S(2)}, u32[]{:S(2)}) %collective-permute-start) | collective-permute-done | bytes 196640 | tf_op jit(solution)/shard_map/ppermute | solution.py:118
  68.3 1.7 %reshape.102 = bf16[16,2,4096]{2,1,0:T(2,128)(2,1)} reshape(bf16[16,16,16,32]{3,2,1,0:T(8,128)(2,1)S(1)} %fusion.74) | data formatting | bytes 524288
  70.0 3.5 %all-to-all-start.2 = ((bf16[16,2,4096]{2,1,0:T(2,128)(2,1)}), bf16[16,2,4096]{2,1,0:T(2,128)(2,1)S(1)}, u32[]{:S(2)}, u32[]{:S(2)}) async-start(bf16[16,2,4096]{2,1,0:T(2,128)(2,1)} %reshape.102), calls=%async_computation.2 | async-start | bytes 524288 | tf_op jit(solution)/shard_map/all_to_all | solution.py:150
  74.3 7.2 %all-to-all-done.2 = bf16[16,2,4096]{2,1,0:T(2,128)(2,1)S(1)} async-done(((bf16[16,2,4096]{2,1,0:T(2,128)(2,1)}), bf16[16,2,4096]{2,1,0:T(2,128)(2,1)S(1)}, u32[]{:S(2)}, u32[]{:S(2)}) %all-to-all-start.2) | async-done | bytes 262176 | tf_op jit(solution)/shard_map/all_to_all | solution.py:150
  81.6 1.5 %reshape.103 = bf16[16,16,16,32]{3,2,1,0:T(8,128)(2,1)} reshape(bf16[16,2,4096]{2,1,0:T(2,128)(2,1)S(1)} %all-to-all-done.2) | data formatting | bytes 524288
  83.0 1.3 %reshape.104 = bf16[16,2,7168]{2,1,0:T(2,128)(2,1)} reshape(bf16[16,14,16,64]{3,2,1,0:T(8,128)(2,1)S(1)} %bitcast.206) | data formatting | bytes 917504
  84.3 4.2 %all-to-all-start.3 = ((bf16[16,2,7168]{2,1,0:T(2,128)(2,1)}), bf16[16,2,7168]{2,1,0:T(2,128)(2,1)}, u32[]{:S(2)}, u32[]{:S(2)}) async-start(bf16[16,2,7168]{2,1,0:T(2,128)(2,1)} %reshape.104), calls=%async_computation.3 | async-start | bytes 917504 | tf_op jit(solution)/shard_map/all_to_all | solution.py:154
  89.6 2.4 %copy.68 = bf16[32,16,256]{2,1,0:T(8,128)(2,1)S(1)} copy(bf16[32,16,256]{0,1,2:T(8,128)(2,1)} %bitcast.201) | data formatting | bytes 524288 | tf_op jit(solution)/shard_map/squeeze | solution.py:150
  92.0 3.4 %fusion.2 = bf16[32,16,1024]{2,1,0:T(8,128)(2,1)} fusion(f32[32,16,1024]{2,0,1:T(8,128)S(1)} %fusion.77, bf16[32,16,1024]{2,1,0:T(8,128)(2,1)S(1)} %copy-done.1, bf16[32,16,256]{2,1,0:T(8,128)(2,1)S(1)} %copy.68, bf16[256,2044]{1,0:T(8,128)(2,1)} %copy-done.2), kind=kOutput, calls=%fused_computation.3 | convolution fusion | flops 271056896 | bytes 4980736 | tf_op jit(solution)/shard_map/qrj,jc->qrc/dot_general | solution.py:151
  95.4 3.3 %all-to-all-done.3 = bf16[16,2,7168]{2,1,0:T(2,128)(2,1)} async-done(((bf16[16,2,7168]{2,1,0:T(2,128)(2,1)}), bf16[16,2,7168]{2,1,0:T(2,128)(2,1)}, u32[]{:S(2)}, u32[]{:S(2)}) %all-to-all-start.3) | async-done | bytes 458784 | tf_op jit(solution)/shard_map/all_to_all | solution.py:154
  98.7 2.1 %reshape.105 = bf16[16,14,16,64]{3,2,1,0:T(8,128)(2,1)S(1)} reshape(bf16[16,2,7168]{2,1,0:T(2,128)(2,1)} %all-to-all-done.3) | data formatting | bytes 917504
  (78 shorter events, 16.1 us)
Async XLA Ops:
  0.6 24.2 %copy-start = (bf16[224,32]{0,1:T(8,128)(2,1)S(1)}, bf16[224,32]{0,1:T(8,128)(2,1)}, u32[]{:S(2)}) copy-start(bf16[224,32]{0,1:T(8,128)(2,1)} %param.6) | copy-start | bytes 43012
  2.5 1.8 %copy-start.1 = (bf16[32,16,1024]{2,1,0:T(8,128)(2,1)S(1)}, bf16[32,16,1024]{2,1,0:T(8,128)(2,1)}, u32[]{:S(2)}) copy-start(bf16[32,16,1024]{2,1,0:T(8,128)(2,1)} %param.5) | copy-start | bytes 3145732
  4.3 1.5 %copy-start.2 = (bf16[256,2044]{1,0:T(8,128)(2,1)}, bf16[256,2044]{1,0:T(8,128)(2,1)S(1)}, u32[]{:S(2)}) copy-start(bf16[256,2044]{1,0:T(8,128)(2,1)S(1)} %reshape.84) | copy-start | bytes 3139588
  7.4 13.8 %all-to-all-start = ((bf16[16,2,4096]{2,1,0:T(2,128)(2,1)}), bf16[16,2,4096]{2,1,0:T(2,128)(2,1)S(1)}, u32[]{:S(2)}, u32[]{:S(2)}) async-start(bf16[16,2,4096]{2,1,0:T(2,128)(2,1)} %reshape.100), calls=%async_computation | async-start | bytes 524288 | tf_op jit(solution)/shard_map/all_to_all | solution.py:96
  14.8 10.0 %copy-start.7 = (bf16[8,224]{1,0:T(8,128)(2,1)S(1)}, bf16[8,224]{1,0:T(8,128)(2,1)}, u32[]{:S(2)}) copy-start(bf16[8,224]{1,0:T(8,128)(2,1)} %param.7) | copy-start | bytes 10756
  17.1 13.1 %copy-start.6 = (bf16[128,764]{1,0:T(8,128)(2,1)}, bf16[128,764]{1,0:T(8,128)(2,1)S(1)}, u32[]{:S(2)}) copy-start(bf16[128,764]{1,0:T(8,128)(2,1)S(1)} %reshape.82) | copy-start | bytes 586756
  21.3 13.7 %all-to-all-start.1 = ((bf16[16,2,7168]{2,1,0:T(2,128)(2,1)}), bf16[16,2,7168]{2,1,0:T(2,128)(2,1)S(1)}, u32[]{:S(2)}, u32[]{:S(2)}) async-start(bf16[16,2,7168]{2,1,0:T(2,128)(2,1)} %reshape.98), calls=%async_computation.1 | async-start | bytes 917504 | tf_op jit(solution)/shard_map/all_to_all | solution.py:70
  35.5 10.0 %copy-start.3 = (f32[32,16,64]{2,1,0:T(8,128)S(1)}, f32[32,16,64]{2,1,0:T(8,128)}, u32[]{:S(2)}) copy-start(f32[32,16,64]{2,1,0:T(8,128)} %get-tuple-element.16) | copy-start | bytes 393220
  36.3 12.2 %slice-start = ((bf16[128,764]{1,0:T(8,128)(2,1)}), bf16[128,256]{1,0:T(8,128)(2,1)S(1)}, s32[]{:S(2)}) async-start(bf16[128,764]{1,0:T(8,128)(2,1)} %copy-done.6), calls=%async_computation.4 | async-start | bytes 131072 | tf_op jit(solution)/shard_map/slice | solution.py:53
  38.0 18.2 %collective-permute-start.1 = (f32[32,16,96]{2,1,0:T(8,128)S(1)}, f32[32,16,96]{2,1,0:T(8,128)S(1)}, u32[]{:S(2)}, u32[]{:S(2)}) collective-permute-start(f32[32,16,96]{2,1,0:T(8,128)S(1)} %pad_maximum_fusion.1), channel_id=1, source_target_pairs={{16,0},{32,16},{48,32},{64,48},{80,64},{96,80},{112,96},{128,112},... | collective-permute-start | bytes 589832 | tf_op jit(solution)/shard_map/ppermute | solution.py:119
  46.4 18.0 %collective-permute-start = (f32[32,16,96]{2,1,0:T(8,128)}, f32[32,16,96]{2,1,0:T(8,128)S(1)}, u32[]{:S(2)}, u32[]{:S(2)}) collective-permute-start(f32[32,16,96]{2,1,0:T(8,128)} %pad_maximum_fusion), channel_id=1, source_target_pairs={{0,16},{16,32},{32,48},{48,64},{64,80},{80,96},{96,112},{112,128},... | collective-permute-start | bytes 589832 | tf_op jit(solution)/shard_map/ppermute | solution.py:118
  56.2 8.3 %copy-start.4 = (f32[32,16,96]{2,1,0:T(8,128)}, f32[32,16,96]{2,1,0:T(8,128)S(1)}, u32[]{:S(2)}) copy-start(f32[32,16,96]{2,1,0:T(8,128)S(1)} %collective-permute-done.1) | copy-start | bytes 589828
  65.1 1.4 %copy-start.5 = (f32[32,16,96]{2,1,0:T(8,128)S(1)}, f32[32,16,96]{2,1,0:T(8,128)}, u32[]{:S(2)}) copy-start(f32[32,16,96]{2,1,0:T(8,128)} %copy-done.4) | copy-start | bytes 589828
  70.0 11.6 %all-to-all-start.2 = ((bf16[16,2,4096]{2,1,0:T(2,128)(2,1)}), bf16[16,2,4096]{2,1,0:T(2,128)(2,1)S(1)}, u32[]{:S(2)}, u32[]{:S(2)}) async-start(bf16[16,2,4096]{2,1,0:T(2,128)(2,1)} %reshape.102), calls=%async_computation.2 | async-start | bytes 524288 | tf_op jit(solution)/shard_map/all_to_all | solution.py:150
  84.3 14.4 %all-to-all-start.3 = ((bf16[16,2,7168]{2,1,0:T(2,128)(2,1)}), bf16[16,2,7168]{2,1,0:T(2,128)(2,1)}, u32[]{:S(2)}, u32[]{:S(2)}) async-start(bf16[16,2,7168]{2,1,0:T(2,128)(2,1)} %reshape.104), calls=%async_computation.3 | async-start | bytes 917504 | tf_op jit(solution)/shard_map/all_to_all | solution.py:154
